TPU v7x, 256 devices: a whole 4x4x8 slice. The times are simulated.
256 devices in a mesh: dp: 64 (over x, y_hi, z), tensor: 4 (over y_lo, core).
Axes of the slice: x: 4, y: 4 (y_hi: 2, y_lo: 2; y = y_hi * 2 + y_lo), z: 8, core: 2. Of those that a mesh axis runs over, the one named last changes fastest.
Arguments:
- residual: bfloat16 [512, 64, 4096], P('dp', None, 'tensor'), may hold values from -128 to 128
- queries: bfloat16 [512, 64, 4096], P('dp', None, 'tensor'), may hold values from -30 to 30
- attn_keys: bfloat16 [512, 64, 512], P('dp', None, 'tensor'), may hold values from -6 to 6
- values: bfloat16 [512, 64, 512], P('dp', None, 'tensor'), may hold values from -6 to 6
- out_weight: bfloat16 [4096, 4096], P('tensor'), may hold values from -0.09375 to 0.09375
- norm_gain: float32 [4096], P('tensor'), may hold values from 0.1 to 1.9
- probe_weight: float32 [4096, 64], P('tensor'), may hold values from -0.09375 to 0.09375
- partner_slot: int32 [512], P('dp'), may hold values from 0 to 7, as said below
- patch_list: int32 [512, 64, 2], P('dp', 'tensor'), may hold values from 0 to 63, as said below
- concept_labels: int32 [512, 64], P('dp'), may hold values from 0 to 63
Outputs:
- attn_out: bfloat16 [512, 64, 4096], P('dp', None, 'tensor')
- logits: float32 [512, 64, 64], P('dp')
- probe_grad: float32 [4096, 64], P('tensor')
Inputs may be any that keep to these rules, and one draw needn't show every extreme that they name: Prompt j of device i of dp, for i below 32, is paired with prompt partner_slot of it on device i + 32, and that prompt's partner_slot is j; on each device the values are a permutation. `patch_list`: each entry is (head, position). A prompt's list equals its partner's, entry for entry. Its entries are distinct, and entries k * 16 to (k + 1) * 16 - 1 name heads of the k-th block of 8 consecutive heads.
All inputs are finite; a program needn't handle non-finite values.
Results may differ from a plain program's by a relative error of at most 0.01.
Values may be sent and summed in bfloat16 or wider, within the bound.
No kernel may reach another device: no remote copies, remote signals or barrier semaphores. Data moves between devices by JAX's collectives and lax.ppermute only.
A program may use at most 128 MiB of HBM per device.

v0:
```python
import math
import jax
import jax.numpy as jnp
from jax import lax
from jax.sharding import PartitionSpec as P

DW = 4096
HDIM = 128
norm_epsilon = 1e-05


def passed_along(block, axis, distance):
    devices = range(lax.axis_size(axis))
    route = [((i - distance) % len(devices), i) for i in devices]
    return lax.ppermute(block, axis, route)


def attend(queries, attn_keys, values):
    prompt_count = queries.shape[0]
    seq_length = queries.shape[1]
    local_kv = attn_keys.shape[2] // HDIM
    local_heads = queries.shape[2] // HDIM
    group_size = local_heads // local_kv
    query_blocks = queries.reshape(prompt_count, seq_length, local_kv, group_size, HDIM)
    key_blocks = attn_keys.reshape(prompt_count, seq_length, local_kv, HDIM)
    value_blocks = values.reshape(prompt_count, seq_length, local_kv, HDIM)
    scores = jnp.einsum(
        "pqkgd,pskd->pkgqs", query_blocks, key_blocks, preferred_element_type=jnp.float32
    ) / math.sqrt(HDIM)
    causal = jnp.arange(seq_length)[:, None] >= jnp.arange(seq_length)[None, :]
    scores = jnp.where(causal, scores, -jnp.inf)
    highest = jnp.max(scores, axis=-1, keepdims=True)
    exponent = jnp.exp(scores - highest)
    weights = (exponent / jnp.sum(exponent, axis=-1, keepdims=True)).astype(jnp.bfloat16)
    mixed_rows = jnp.einsum(
        "pkgqs,pskd->pqkgd", weights, value_blocks, preferred_element_type=jnp.float32
    )
    return mixed_rows.astype(jnp.bfloat16).reshape(prompt_count, seq_length, local_heads, HDIM)


def per_device(
    residual,
    queries,
    attn_keys,
    values,
    out_weight,
    norm_gain,
    probe_weight,
    partner_slot,
    patch_list,
    concept_labels,
):
    prompt_count = residual.shape[0]
    seq_length = residual.shape[1]
    feature_count = residual.shape[2]
    token_count = prompt_count * seq_length
    heads_out = attend(queries, attn_keys, values)
    local_heads = heads_out.shape[2]
    head_ids = patch_list[..., 0] % local_heads
    pos_ids = patch_list[..., 1]
    row_ids = jnp.broadcast_to(jnp.arange(prompt_count, dtype=jnp.int32)[:, None], head_ids.shape)
    patch_mask = (
        jnp.zeros((prompt_count, seq_length, local_heads), dtype=bool)
        .at[row_ids, pos_ids, head_ids]
        .set(True)
    )
    half_way = lax.axis_size("dp") // 2
    arrived = passed_along(heads_out, "dp", half_way)
    entry_values = arrived[partner_slot][row_ids, pos_ids, head_ids]
    incoming = jnp.zeros_like(heads_out).at[row_ids, pos_ids, head_ids].set(entry_values)
    patched = jnp.where(patch_mask[..., None], incoming, heads_out)
    partial_value = jnp.dot(
        patched.reshape(token_count, -1), out_weight, preferred_element_type=jnp.float32
    )
    attn_local = lax.psum_scatter(
        partial_value.astype(jnp.bfloat16), "tensor", scatter_dimension=1, tiled=True
    )
    hidden = residual.reshape(token_count, feature_count).astype(jnp.float32) + attn_local.astype(
        jnp.float32
    )
    square_local = jnp.sum(hidden * hidden, axis=1)
    scaled = hidden * norm_gain
    square_sum = lax.psum(square_local, "tensor")
    inverse_rms = lax.rsqrt(square_sum / DW + norm_epsilon)
    normed = scaled * inverse_rms[:, None]
    logit_part = jnp.dot(
        normed, probe_weight, precision=lax.Precision.HIGHEST, preferred_element_type=jnp.float32
    )
    logits = lax.psum(logit_part.astype(jnp.bfloat16), "tensor").astype(jnp.float32)
    classes = jnp.arange(probe_weight.shape[1], dtype=jnp.int32)
    target = (concept_labels.reshape(token_count)[:, None] == classes[None, :]).astype(jnp.float32)
    error = jax.nn.sigmoid(logits) - target
    total_tokens = token_count * lax.axis_size("dp")
    grad_local = lax.dot_general(
        normed,
        error,
        (((0,), (0,)), ((), ())),
        precision=lax.Precision.HIGHEST,
        preferred_element_type=jnp.float32,
    ) / math.sqrt(total_tokens)
    probe_grad = lax.psum(grad_local, "dp")
    return (
        attn_local.reshape(prompt_count, seq_length, feature_count),
        logits.reshape(prompt_count, seq_length, -1),
        probe_grad,
    )


def solution(mesh):
    return jax.shard_map(
        per_device,
        mesh=mesh,
        in_specs=(
            P("dp", None, "tensor"),
            P("dp", None, "tensor"),
            P("dp", None, "tensor"),
            P("dp", None, "tensor"),
            P("tensor", None),
            P("tensor"),
            P("tensor", None),
            P("dp"),
            P("dp", "tensor", None),
            P("dp", None),
        ),
        out_specs=(P("dp", None, "tensor"), P("dp", None, None), P("tensor", None)),
        check_vma=False,
    )
```

profile of v0, /device:TPU:8, one launch (start us, length us, event | category | flops | bytes accessed | tf_op | source)
XLA Modules:
  0.0 822.0 jit_solution(9259078480574834374)
XLA Ops:
  7.2 0.0 reduce-scatter.2.cloned.1.call-start
  7.2 1.2 copy-done
  8.4 2.1 fusion.33
  10.5 0.5 fusion
  11.0 0.6 fusion.3
  11.7 3.1 collective-permute-start
  14.8 0.5 broadcast.168
  15.3 0.7 fusion.32
  16.0 0.1 reshape.81
  16.1 0.1 reshape.87
  16.2 8.5 %scatter_fusion = pred[8,64,8]{1,2,0:T(8,128)(4,1)S(1)} fusion(pred[8,64,8]{1,2,0:T(8,128)(4,1)S(1)} %broadcast_in_dim.23, s32[128]{0:T(128)S(1)} %reshape.87, pred[128]{0:T(512)(128)(4,1)S(1)} %broadcast.130), kind=kCustom, calls=%fused_computation.2 | custom fusion | bytes 1920 | tf_op jit(solution)/shard_map/scatter | solution.py:65
  24.8 13.4 %collective-permute-done = bf16[8,64,8,128]{3,1,2,0:T(8,128)(2,1)S(1)} collective-permute-done((bf16[8,64,8,128]{3,1,2,0:T(8,128)(2,1)S(1)}, bf16[8,64,8,128]{3,1,2,0:T(8,128)(2,1)S(1)}, u32[]{:S(2)}, u32[]{:S(2)}) %collective-permute-start) | collective-permute-done | bytes 1048608 | tf_op jit(solution)/shard_map/ppermute | solution.py:15
  38.2 0.7 gather_fusion
  38.9 0.7 copy.19
  39.6 1.2 gather_fusion.1
  40.9 0.1 broadcast_in_dim.27
  41.0 8.0 scatter_fusion.1
  49.0 1.8 copy_select_fusion
  50.8 0.7 copy.21
  51.5 9.4 %convolution_convert_fusion = bf16[512,4096]{1,0:T(8,128)(2,1)} fusion(bf16[1024,4096]{1,0:T(8,128)(2,1)} %param.14, bf16[64,8,8,128]{3,2,1,0:T(8,128)(2,1)S(1)} %bitcast.52), kind=kOutput, calls=%fused_computation.4 | convolution fusion | flops 4297064448 | bytes 13631488 | tf_op jit(solution)/shard_map/dot_general | solution.py:72
  61.0 0.0 all-reduce.3.cloned.1.call-start
  61.0 49.1 %reduce-scatter.2.cloned.1.call-done = bf16[512,1024]{1,0:T(8,128)(2,1)} async-done(((bf16[512,4096]{1,0:T(8,128)(2,1)}), bf16[512,1024]{1,0:T(8,128)(2,1)}) %reduce-scatter.2.cloned.1.call-update) | async-done | bytes 1048592 | tf_op jit(solution)/shard_map/reduce_scatter | solution.py:75
  110.2 1.7 multiply_reduce_fusion
  111.9 7.7 psum.21
  119.7 3.1 fusion.5
  122.8 0.0 all-reduce.5.cloned.1.call-start
  122.9 0.1 eq.17
  122.9 40.9 %all-reduce.3.cloned.1.call-done = bf16[512,64]{0,1:T(8,128)(2,1)} async-done(((bf16[512,64]{0,1:T(8,128)(2,1)}), bf16[512,64]{0,1:T(8,128)(2,1)}) %all-reduce.3.cloned.1.call-update) | async-done | bytes 65552 | tf_op jit(solution)/shard_map/psum | solution.py:89
  163.9 3.5 fusion.4
  167.4 0.8 copy.26
  168.2 645.6 %all-reduce.5.cloned.1.call-done = f32[1024,64]{0,1:T(8,128)} async-done(((f32[1024,64]{0,1:T(8,128)}), f32[1024,64]{0,1:T(8,128)}) %all-reduce.5.cloned.1.call-update) | async-done | bytes 262160 | tf_op jit(solution)/shard_map/psum | solution.py:101
  813.8 1.7 copy.44
  (31 shorter events, 0.2 us)
Async XLA Ops:
  7.2 1.2 copy-start
  7.2 103.0 %reduce-scatter.2.cloned.1.call-start = ((), (), s32[]{:S(2)}) async-start(), calls=%async_computation.1 | async-start | bytes 5242880 | tf_op jit(solution)/shard_map/reduce_scatter | solution.py:75
  8.4 2.6 copy-start.8
  11.0 3.8 copy-start.5
  11.7 13.1 %copy-start.1 = (bf16[8,64,8,128]{3,1,2,0:T(8,128)(2,1)}, bf16[8,64,8,128]{3,1,2,0:T(8,128)(2,1)S(1)}, u32[]{:S(2)}) copy-start(bf16[8,64,8,128]{3,1,2,0:T(8,128)(2,1)S(1)} %fusion.3) | copy-start | bytes 3145732
  11.7 13.0 %copy-start.10 = (s32[8]{0:T(128)S(1)}, s32[8]{0:T(128)}, u32[]{:S(2)}) copy-start(s32[8]{0:T(128)} %param.17) | copy-start | bytes 100
  11.7 26.5 %collective-permute-start = (bf16[8,64,8,128]{3,1,2,0:T(8,128)(2,1)S(1)}, bf16[8,64,8,128]{3,1,2,0:T(8,128)(2,1)S(1)}, u32[]{:S(2)}, u32[]{:S(2)}) collective-permute-start(bf16[8,64,8,128]{3,1,2,0:T(8,128)(2,1)S(1)} %fusion.3), channel_id=1, source_target_pairs={{128,0},{132,4},{136,8},{140,12},{144,16},{148,20},{152,24},{156,2... | collective-permute-start | bytes 3145736 | tf_op jit(solution)/shard_map/ppermute | solution.py:15
  60.9 49.3 %copy-start.2 = (bf16[8,64,1024]{2,1,0:T(8,128)(2,1)S(1)}, bf16[8,64,1024]{2,1,0:T(8,128)(2,1)}, u32[]{:S(2)}) copy-start(bf16[8,64,1024]{2,1,0:T(8,128)(2,1)} %param.10) | copy-start | bytes 3145732
  60.9 58.7 %copy-start.7 = (f32[1024,64]{0,1:T(8,128)S(1)}, f32[1024,64]{0,1:T(8,128)}, u32[]{:S(2)}) copy-start(f32[1024,64]{0,1:T(8,128)} %param.16) | copy-start | bytes 786436
  60.9 58.7 %copy-start.9 = (f32[1024]{0:T(1024)S(1)}, f32[1024]{0:T(1024)}, u32[]{:S(2)}) copy-start(f32[1024]{0:T(1024)} %param.15) | copy-start | bytes 12292
  60.9 61.9 %copy-start.6 = (s32[8,64]{1,0:T(8,128)S(1)}, s32[8,64]{1,0:T(8,128)}, u32[]{:S(2)}) copy-start(s32[8,64]{1,0:T(8,128)} %param.19) | copy-start | bytes 6148
  61.0 102.9 %all-reduce.3.cloned.1.call-start = ((), (), s32[]{:S(2)}) async-start(), calls=%async_computation.2 | async-start | bytes 131072 | tf_op jit(solution)/shard_map/psum | solution.py:89
  110.2 9.5 %copy-start.3 = (bf16[512,1024]{1,0:T(8,128)(2,1)S(1)}, bf16[512,1024]{1,0:T(8,128)(2,1)}, u32[]{:S(2)}) copy-start(bf16[512,1024]{1,0:T(8,128)(2,1)} %reduce-scatter.2.cloned.1.call-done) | copy-start | bytes 3145732
  122.8 691.0 %all-reduce.5.cloned.1.call-start = ((), (), s32[]{:S(2)}) async-start(), calls=%async_computation.3 | async-start | bytes 524288 | tf_op jit(solution)/shard_map/psum | solution.py:101
  163.9 3.5 copy-start.4
Sparse Core Ops, SparseCore 0:
  61.0 49.0 reduce-scatter.1
  122.9 40.9 all-reduce.2
  167.5 646.2 all-reduce.4
where the time goes:
time: 822 us
  waiting for transfers between devices  749 us (91%)
  local copies, waits for them, and re-layouts  24.4 us (3%)
  matrix products  18.7 us (2%)
  between operations  14 us (2%)
    psum x1, waiting for transfers between devices, per_device(): probe_grad = lax.psum(grad_local, 'dp')  646 us
    reduce_scatter x1, waiting for transfers between devices, per_device(): lax.psum_scatter(partial_value.astype(jnp.bfloat16), 'tensor', scatter_di...  49.1 us
    psum x1, waiting for transfers between devices, per_device(): lax.psum(logit_part.astype(jnp.bfloat16), 'tensor').astype(jnp.float32)  40.9 us
  transfers between devices with their start and end apart: 4, of which 4 were waited for; matrix products, arithmetic and copies ran while one was open for 1% of the time, Pallas kernels for 0%

commit v1 on v0

--- a/solution.py
+++ b/solution.py
@@ -86,7 +86,9 @@
     logit_part = jnp.dot(
         normed, probe_weight, precision=lax.Precision.HIGHEST, preferred_element_type=jnp.float32
     )
-    logits = lax.psum(logit_part.astype(jnp.bfloat16), "tensor").astype(jnp.float32)
+    logits = jnp.sum(lax.all_gather(logit_part.astype(jnp.bfloat16), "tensor"), 0).astype(
+        jnp.float32
+    )
     classes = jnp.arange(probe_weight.shape[1], dtype=jnp.int32)
     target = (concept_labels.reshape(token_count)[:, None] == classes[None, :]).astype(jnp.float32)
     error = jax.nn.sigmoid(logits) - target

time: 822 us -> 787 us (0.957)
  waiting for transfers between devices: 749 us -> 707 us
    psum x1 -> x0, waiting for transfers between devices: 40.9 us -> none  [per_device(): lax.psum(logit_part.astype(jnp.bfloat16), 'tensor').astype(jnp.float32)]
  transfers between devices with their start and end apart: 4 -> 3, of which waited for: 4 -> 3; matrix products, arithmetic and copies ran while one was open for 1% -> 1% of each run, Pallas kernels for 0% -> 0%
where the time goes in v1:
time: 787 us
  waiting for transfers between devices  707 us (90%)
  local copies, waits for them, and re-layouts  26.2 us (3%)
  matrix products  17.1 us (2%)
  between operations  14.2 us (2%)
  blocking collectives  14 us (2%)
    psum x1, waiting for transfers between devices, per_device(): probe_grad = lax.psum(grad_local, 'dp')  645 us
    reduce_scatter x1, waiting for transfers between devices, per_device(): lax.psum_scatter(partial_value.astype(jnp.bfloat16), 'tensor', scatter_di...  48.5 us
  transfers between devices with their start and end apart: 3, of which 3 were waited for; matrix products, arithmetic and copies ran while one was open for 1% of the time, Pallas kernels for 0%

profile of v1, /device:TPU:8, one launch (start us, length us, event | category | flops | bytes accessed | tf_op | source)
XLA Modules:
  0.0 786.6 jit_solution(3456478017747611399)
XLA Ops:
  7.2 1.2 copy-done
  8.4 2.1 fusion.33
  10.5 0.5 fusion
  11.0 0.6 fusion.3
  11.7 3.1 collective-permute-start
  14.8 0.5 broadcast.168
  15.4 0.7 fusion.32
  16.0 0.1 reshape.82
  16.1 0.1 reshape.88
  16.2 8.5 %scatter_fusion = pred[8,64,8]{1,2,0:T(8,128)(4,1)S(1)} fusion(pred[8,64,8]{1,2,0:T(8,128)(4,1)S(1)} %broadcast_in_dim.23, s32[128]{0:T(128)S(1)} %reshape.88, pred[128]{0:T(512)(128)(4,1)S(1)} %broadcast.130), kind=kCustom, calls=%fused_computation.2 | custom fusion | bytes 1920 | tf_op jit(solution)/shard_map/scatter | solution.py:65
  24.8 13.4 %collective-permute-done = bf16[8,64,8,128]{3,1,2,0:T(8,128)(2,1)S(1)} collective-permute-done((bf16[8,64,8,128]{3,1,2,0:T(8,128)(2,1)S(1)}, bf16[8,64,8,128]{3,1,2,0:T(8,128)(2,1)S(1)}, u32[]{:S(2)}, u32[]{:S(2)}) %collective-permute-start) | collective-permute-done | bytes 1048608 | tf_op jit(solution)/shard_map/ppermute | solution.py:15
  38.2 0.7 gather_fusion
  38.9 0.7 copy.23
  39.6 1.2 gather_fusion.1
  40.9 0.1 broadcast_in_dim.27
  41.0 8.0 %scatter_fusion.1 = bf16[8,64,8,128]{3,2,1,0:T(8,128)(2,1)S(1)} fusion(bf16[8,64,8,128]{3,2,1,0:T(8,128)(2,1)S(1)} %broadcast_in_dim.27, s32[128]{0:T(128)S(1)} %reshape.88, bf16[128,128]{1,0:T(8,128)(2,1)S(1)} %gather_fusion.1), kind=kCustom, calls=%fused_computation.3 | custom fusion | bytes 99840 | tf_op jit(solution)/shard_map/scatter | solution.py:70
  49.0 1.8 copy_select_fusion
  50.8 0.7 copy.25
  51.5 9.4 %convolution_convert_fusion = bf16[512,4096]{1,0:T(8,128)(2,1)} fusion(bf16[1024,4096]{1,0:T(8,128)(2,1)} %param.14, bf16[64,8,8,128]{3,2,1,0:T(8,128)(2,1)S(1)} %bitcast.54), kind=kOutput, calls=%fused_computation.4 | convolution fusion | flops 4297064448 | bytes 13631488 | tf_op jit(solution)/shard_map/dot_general | solution.py:72
  61.0 0.6 copy-done.5
  61.6 0.1 eq.17
  61.7 48.5 %reduce-scatter.2.cloned.1.call-done = bf16[512,1024]{1,0:T(8,128)(2,1)} async-done(((bf16[512,4096]{1,0:T(8,128)(2,1)}), bf16[512,1024]{1,0:T(8,128)(2,1)}) %reduce-scatter.2.cloned.1.call-update) | async-done | bytes 1048592 | tf_op jit(solution)/shard_map/reduce_scatter | solution.py:75
  110.2 1.7 multiply_reduce_fusion
  111.9 7.7 psum.14
  119.7 2.5 fusion.5
  122.1 6.2 all-gather
  128.4 1.1 reshape.100
  129.5 0.3 reduce_sum.32
  129.8 2.6 fusion.4
  132.4 0.8 copy.30
  133.2 644.9 %all-reduce.2.cloned.1.call-done = f32[1024,64]{0,1:T(8,128)} async-done(((f32[1024,64]{0,1:T(8,128)}), f32[1024,64]{0,1:T(8,128)}) %all-reduce.2.cloned.1.call-update) | async-done | bytes 262160 | tf_op jit(solution)/shard_map/psum | solution.py:103
  778.1 1.7 copy.47
  (29 shorter events, 0.2 us)
Async XLA Ops:
  7.2 1.2 copy-start
  7.2 103.0 %reduce-scatter.2.cloned.1.call-start = ((), (), s32[]{:S(2)}) async-start(), calls=%async_computation.1 | async-start | bytes 5242880 | tf_op jit(solution)/shard_map/reduce_scatter | solution.py:75
  8.4 2.6 copy-start.7
  11.0 3.8 copy-start.4
  11.7 13.1 %copy-start.1 = (bf16[8,64,8,128]{3,1,2,0:T(8,128)(2,1)}, bf16[8,64,8,128]{3,1,2,0:T(8,128)(2,1)S(1)}, u32[]{:S(2)}) copy-start(bf16[8,64,8,128]{3,1,2,0:T(8,128)(2,1)S(1)} %fusion.3) | copy-start | bytes 3145732
  11.7 13.0 %copy-start.9 = (s32[8]{0:T(128)S(1)}, s32[8]{0:T(128)}, u32[]{:S(2)}) copy-start(s32[8]{0:T(128)} %param.17) | copy-start | bytes 100
  11.7 26.5 %collective-permute-start = (bf16[8,64,8,128]{3,1,2,0:T(8,128)(2,1)S(1)}, bf16[8,64,8,128]{3,1,2,0:T(8,128)(2,1)S(1)}, u32[]{:S(2)}, u32[]{:S(2)}) collective-permute-start(bf16[8,64,8,128]{3,1,2,0:T(8,128)(2,1)S(1)} %fusion.3), channel_id=1, source_target_pairs={{128,0},{132,4},{136,8},{140,12},{144,16},{148,20},{152,24},{156,2... | collective-permute-start | bytes 3145736 | tf_op jit(solution)/shard_map/ppermute | solution.py:15
  60.9 0.7 copy-start.5
  60.9 49.3 %copy-start.2 = (bf16[8,64,1024]{2,1,0:T(8,128)(2,1)S(1)}, bf16[8,64,1024]{2,1,0:T(8,128)(2,1)}, u32[]{:S(2)}) copy-start(bf16[8,64,1024]{2,1,0:T(8,128)(2,1)} %param.10) | copy-start | bytes 3145732
  60.9 58.7 %copy-start.6 = (f32[1024,64]{0,1:T(8,128)S(1)}, f32[1024,64]{0,1:T(8,128)}, u32[]{:S(2)}) copy-start(f32[1024,64]{0,1:T(8,128)} %param.16) | copy-start | bytes 786436
  60.9 58.7 %copy-start.8 = (f32[1024]{0:T(1024)S(1)}, f32[1024]{0:T(1024)}, u32[]{:S(2)}) copy-start(f32[1024]{0:T(1024)} %param.15) | copy-start | bytes 12292
  60.9 717.2 %all-reduce.2.cloned.1.call-start = ((), (), s32[]{:S(2)}) async-start(), calls=%async_computation.2 | async-start | bytes 524288 | tf_op jit(solution)/shard_map/psum | solution.py:103
  110.2 9.5 %copy-start.3 = (bf16[512,1024]{1,0:T(8,128)(2,1)S(1)}, bf16[512,1024]{1,0:T(8,128)(2,1)}, u32[]{:S(2)}) copy-start(bf16[512,1024]{1,0:T(8,128)(2,1)} %reduce-scatter.2.cloned.1.call-done) | copy-start | bytes 3145732
Sparse Core Ops, SparseCore 0:
  61.0 49.0 reduce-scatter.1
  132.5 645.5 all-reduce.1
